TPU v7x, 512 devices: a whole 4x8x8 slice. The times are simulated.
512 devices in a mesh: dp: 16 (over z, core), ctx: 32 (over y, x).
Axes of the slice: x: 4, y: 8, z: 8, core: 2. Of those that a mesh axis runs over, the one named last changes fastest.
Arguments:
- positions: int32 [49152], P('dp'), parts along dimension 0, may hold values from 0 to 24575, as said below
- queries: bfloat16 [147456, 2048], P(('dp', 'ctx')), parts along dimension 0, may hold values from -12 to 12
- keys_values: bfloat16 [147456, 1024], P(('dp', 'ctx')), parts along dimension 0, may hold values from -12 to 12
- router_weight: bfloat16 [147456], P(('dp', 'ctx')), parts along dimension 0, may hold values from 0.25 to 2
Outputs:
- attended: bfloat16 [147456, 2048], P(('dp', 'ctx')), parts along dimension 0
There are 16 independent parts, one for each index of `dp`. A program takes and returns all parts, laid end to end along the dimension named above; each array names one. Nothing has to cross between parts.
Inputs may be any that keep to these rules, and one draw needn't show every extreme that they name: Distinct and increasing. The shard of positions d * 768 to (d + 1) * 768 - 1 holds at most 288 of them, and one shard holds exactly 288; slots of device d's blocks beyond counts[d] hold data that no output reads.
All inputs are finite; a program needn't handle non-finite values.
Results may differ from a plain program's by a relative error of at most 0.0085.
Values may be sent and summed in bfloat16 or wider, within the bound.
No kernel may reach another device: no remote copies, remote signals or barrier semaphores. Data moves between devices by JAX's collectives and lax.ppermute only.
A program may use at most 64 MiB of HBM per device.

v0:
```python
import math
import jax
import jax.numpy as jnp
from jax import lax
from jax.sharding import PartitionSpec as P

QUERY_HEADS = 16
KEY_VALUE_HEADS = 4
HEAD_SIZE = 128
SEL_DEV = 96
TOK_DEV = 768
CAP = 288
large_negative_fill = -1e30


def shard_offsets(positions, devices_ctx):
    bounds = jnp.arange(devices_ctx + 1, dtype=jnp.int32) * TOK_DEV
    return jnp.sum((positions[None, :] < bounds[:, None]).astype(jnp.int32), axis=1)


def pack_forward(arrays, offsets, my_rank, devices_ctx, pair_slots):
    my_start = offsets[my_rank]
    my_count = offsets[my_rank + 1] - my_start
    target = jnp.arange(devices_ctx, dtype=jnp.int32)[:, None]
    slot_index = jnp.arange(pair_slots, dtype=jnp.int32)[None, :]
    global_idx = (my_start // devices_ctx + slot_index) * devices_ctx + target
    local_idx = global_idx - my_start
    usable = ((local_idx >= 0) & (local_idx < my_count)).reshape(-1)
    picked = jnp.clip(local_idx, 0, CAP - 1).reshape(-1)
    result = []
    for member in arrays:
        gathered_rows = jnp.take(member, picked, axis=0)
        mask_shape = usable.reshape(usable.shape + (1,) * (gathered_rows.ndim - 1))
        gathered_rows = jnp.where(mask_shape, gathered_rows, jnp.zeros_like(gathered_rows))
        result.append(gathered_rows.reshape((devices_ctx, pair_slots) + member.shape[1:]))
    return tuple(result)


def unpack_forward(received, offsets, my_rank, devices_ctx, pair_slots):
    slot_ids = jnp.arange(SEL_DEV, dtype=jnp.int32)
    global_idx = slot_ids * devices_ctx + my_rank
    owners = jnp.sum((offsets[None, 1:] <= global_idx[:, None]).astype(jnp.int32), axis=1)
    slot_index = slot_ids - jnp.take(offsets, owners) // devices_ctx
    picked = owners * pair_slots + slot_index
    return tuple(
        (jnp.take(member.reshape((-1,) + member.shape[2:]), picked, axis=0) for member in received)
    )


def pack_return(scaled, offsets, my_rank, devices_ctx, pair_slots):
    starts = offsets[:-1][:, None]
    ends = offsets[1:][:, None]
    slot_index = jnp.arange(pair_slots, dtype=jnp.int32)[None, :]
    local_idx = starts // devices_ctx + slot_index
    global_idx = local_idx * devices_ctx + my_rank
    usable = ((local_idx < SEL_DEV) & (global_idx >= starts) & (global_idx < ends)).reshape(-1)
    picked = jnp.clip(local_idx, 0, SEL_DEV - 1).reshape(-1)
    gathered_rows = jnp.take(scaled, picked, axis=0)
    gathered_rows = jnp.where(usable[:, None], gathered_rows, jnp.zeros_like(gathered_rows))
    return gathered_rows.reshape(devices_ctx, pair_slots, scaled.shape[1])


def unpack_return(received, offsets, my_rank, devices_ctx, pair_slots):
    my_start = offsets[my_rank]
    my_count = offsets[my_rank + 1] - my_start
    slot_ids = jnp.arange(CAP, dtype=jnp.int32)
    global_idx = my_start + slot_ids
    live_slot = slot_ids < my_count
    source = global_idx % devices_ctx
    slot_index = jnp.clip(global_idx // devices_ctx - my_start // devices_ctx, 0, pair_slots - 1)
    flat = received.reshape(-1, received.shape[2])
    gathered_rows = jnp.take(flat, source * pair_slots + slot_index, axis=0)
    return jnp.where(live_slot[:, None], gathered_rows, jnp.zeros_like(gathered_rows))


def block_divisions(rows_total):
    for num_blocks in range(1, rows_total + 1):
        if rows_total % num_blocks == 0 and rows_total // num_blocks <= 512:
            return num_blocks
    return rows_total


def attend(query_row_count, query_index, kv_bal, devices_ctx):
    query_row_total = query_row_count.shape[0]
    group_count = QUERY_HEADS // KEY_VALUE_HEADS
    grouped_heads = query_row_count.reshape(
        query_row_total, KEY_VALUE_HEADS, group_count, HEAD_SIZE
    )
    score_scale = 1.0 / math.sqrt(HEAD_SIZE)

    def update(running, key_block_start, block_start):
        max_run, total_run, accum = running
        key_total_count = key_block_start.shape[0]
        key_rows = block_start + jnp.arange(key_total_count, dtype=jnp.int32)
        key_index = key_rows % SEL_DEV * devices_ctx + key_rows // SEL_DEV
        block_key_rows = key_block_start[:, : KEY_VALUE_HEADS * HEAD_SIZE].reshape(
            key_total_count, KEY_VALUE_HEADS, HEAD_SIZE
        )
        block_value_rows = key_block_start[:, KEY_VALUE_HEADS * HEAD_SIZE :].reshape(
            key_total_count, KEY_VALUE_HEADS, HEAD_SIZE
        )
        scores = (
            jnp.einsum(
                "qkgd,ckd->kgqc", grouped_heads, block_key_rows, preferred_element_type=jnp.float32
            )
            * score_scale
        )
        visible = key_index[None, :] <= query_index[:, None]
        scores = jnp.where(visible, scores, large_negative_fill)
        max_new = jnp.maximum(max_run, jnp.max(scores, axis=-1))
        weights = jnp.where(visible, jnp.exp(scores - max_new[..., None]), 0.0)
        factor = jnp.exp(max_run - max_new)
        total_new = total_run * factor + jnp.sum(weights, axis=-1)
        weighted = jnp.einsum(
            "kgqc,ckd->qkgd",
            weights.astype(jnp.bfloat16),
            block_value_rows,
            preferred_element_type=jnp.float32,
        )
        accum_new = accum * jnp.transpose(factor, (2, 0, 1))[..., None] + weighted
        return (max_new, total_new, accum_new)

    def fold_piece(running, piece_rows, piece_start):
        num_blocks = block_divisions(piece_rows.shape[0])
        if num_blocks == 1:
            return update(running, piece_rows, piece_start)
        block_rows = piece_rows.shape[0] // num_blocks
        blocks = piece_rows.reshape(num_blocks, block_rows, piece_rows.shape[1])

        def scan_step(running_in, inputs_in):
            key_block_start, order_id = inputs_in
            return (update(running_in, key_block_start, piece_start + order_id * block_rows), None)

        running_out, unused = lax.scan(
            scan_step, running, (blocks, jnp.arange(num_blocks, dtype=jnp.int32))
        )
        return running_out

    initial = (
        jnp.full((KEY_VALUE_HEADS, group_count, query_row_total), large_negative_fill, jnp.float32),
        jnp.zeros((KEY_VALUE_HEADS, group_count, query_row_total), jnp.float32),
        jnp.zeros((query_row_total, KEY_VALUE_HEADS, group_count, HEAD_SIZE), jnp.float32),
    )
    max_run, total_run, accum = fold_piece(
        initial, lax.all_gather(kv_bal, "ctx", axis=0, tiled=True), jnp.int32(0)
    )
    result = accum / jnp.transpose(total_run, (2, 0, 1))[..., None]
    return result.reshape(query_row_total, QUERY_HEADS * HEAD_SIZE)


def per_device(positions, queries, keys_values, router_weight):
    devices_ctx = lax.axis_size("ctx")
    my_rank = lax.axis_index("ctx")
    pair_slots = (CAP + devices_ctx - 1) // devices_ctx + 1
    offsets = shard_offsets(positions, devices_ctx)
    packed = pack_forward(
        (queries, keys_values, router_weight), offsets, my_rank, devices_ctx, pair_slots
    )
    moved = (
        lax.all_to_all(packed[0], "ctx", split_axis=0, concat_axis=0, tiled=True),
        lax.all_to_all(packed[1], "ctx", split_axis=0, concat_axis=0, tiled=True),
        lax.all_to_all(packed[2], "ctx", split_axis=0, concat_axis=0, tiled=True),
    )
    query_bal, kv_bal, gate_bal = unpack_forward(moved, offsets, my_rank, devices_ctx, pair_slots)
    query_index = jnp.arange(SEL_DEV, dtype=jnp.int32) * devices_ctx + my_rank
    attended = attend(query_bal, query_index, kv_bal, devices_ctx)
    scaled = (gate_bal.astype(jnp.float32)[:, None] * attended).astype(jnp.bfloat16)
    outgoing = pack_return(scaled, offsets, my_rank, devices_ctx, pair_slots)
    returned = lax.all_to_all(outgoing, "ctx", split_axis=0, concat_axis=0, tiled=True)
    return unpack_return(returned, offsets, my_rank, devices_ctx, pair_slots)


def solution(mesh):
    in_specs = (P("dp"), P(("dp", "ctx"), None), P(("dp", "ctx"), None), P(("dp", "ctx")))
    out_specs = P(("dp", "ctx"), None)
    return jax.shard_map(
        per_device, mesh=mesh, in_specs=in_specs, out_specs=out_specs, check_vma=False
    )
```

profile of v0, /device:TPU:16, one launch (start us, length us, event | category | flops | bytes accessed | tf_op | source)
XLA Modules:
  0.0 319.8 jit_solution(5905198751178517340)
XLA Ops:
  6.5 1.1 convert_reduce_fusion
  12.8 3.6 %gather_fusion.1 = bf16[320]{0:T(512)(128)(2,1)S(1)} fusion(bf16[288]{0:T(512)(128)(2,1)} %param.9, s32[1024]{0:T(1024)S(1)} %pad_clamp_fusion.3), kind=kCustom, calls=%fused_computation.1 | custom fusion | bytes 2560 | tf_op jit(solution)/shard_map/jit(_take)/gather | solution.py:32
  17.8 10.1 %all-to-all-start = ((bf16[32,1,10]{2,1,0:T(2,128)(2,1)}), bf16[32,1,10]{2,1,0:T(2,128)(2,1)S(1)}, u32[]{:S(2)}, u32[]{:S(2)}) async-start(bf16[32,1,10]{2,1,0:T(2,128)(2,1)} %copy.20), calls=%async_computation | async-start | bytes 32768 | tf_op jit(solution)/shard_map/all_to_all | solution.py:162
  28.5 2.1 gather_fusion.3
  30.9 1.2 select_select_fusion.3
  32.1 3.6 %all-to-all-done = bf16[32,1,10]{2,1,0:T(2,128)(2,1)S(1)} async-done(((bf16[32,1,10]{2,1,0:T(2,128)(2,1)}), bf16[32,1,10]{2,1,0:T(2,128)(2,1)S(1)}, u32[]{:S(2)}, u32[]{:S(2)}) %all-to-all-start) | async-done | bytes 672 | tf_op jit(solution)/shard_map/all_to_all | solution.py:162
  35.6 6.2 %all-to-all-start.1 = ((bf16[32,10,1024]{2,1,0:T(8,128)(2,1)}), bf16[32,10,1024]{2,1,0:T(8,128)(2,1)S(1)}, u32[]{:S(2)}, u32[]{:S(2)}) async-start(bf16[32,10,1024]{2,1,0:T(8,128)(2,1)} %select_select_fusion.3), calls=%async_computation.1 | async-start | bytes 2097152 | tf_op jit(solution)/shard_map/all_to_all | solution.py:161
  42.1 1.2 gather_fusion
  43.5 1.3 gather_fusion.2
  44.8 24.6 %all-to-all-done.1 = bf16[32,10,1024]{2,1,0:T(8,128)(2,1)S(1)} async-done(((bf16[32,10,1024]{2,1,0:T(8,128)(2,1)}), bf16[32,10,1024]{2,1,0:T(8,128)(2,1)S(1)}, u32[]{:S(2)}, u32[]{:S(2)}) %all-to-all-start.1) | async-done | bytes 655392 | tf_op jit(solution)/shard_map/all_to_all | solution.py:161
  69.7 0.8 gather_fusion.4
  70.5 0.8 broadcast_select_fusion
  71.3 3.0 gather_fusion.5
  74.3 2.3 gather.57
  76.6 1.7 select_select_fusion.1
  78.3 5.5 %all-to-all-start.2 = ((bf16[32,10,2048]{2,1,0:T(8,128)(2,1)}), bf16[32,10,2048]{2,1,0:T(8,128)(2,1)}, u32[]{:S(2)}, u32[]{:S(2)}) async-start(bf16[32,10,2048]{2,1,0:T(8,128)(2,1)} %select_select_fusion.1), calls=%async_computation.2 | async-start | bytes 4194304 | tf_op jit(solution)/shard_map/all_to_all | solution.py:160
  84.2 56.0 %all-to-all-done.2 = bf16[32,10,2048]{2,1,0:T(8,128)(2,1)} async-done(((bf16[32,10,2048]{2,1,0:T(8,128)(2,1)}), bf16[32,10,2048]{2,1,0:T(8,128)(2,1)}, u32[]{:S(2)}, u32[]{:S(2)}) %all-to-all-start.2) | async-done | bytes 1310752 | tf_op jit(solution)/shard_map/all_to_all | solution.py:160
  140.2 2.5 reshape.582
  142.7 0.8 gather_fusion.6
  143.8 0.8 copy_select_fusion
  144.6 30.1 %all-gather.2.cloned.1.call-done = bf16[3072,1024]{1,0:T(8,128)(2,1)} async-done(((bf16[96,1024]{1,0:T(8,128)(2,1)}), bf16[3072,1024]{1,0:T(8,128)(2,1)}) %all-gather.2.cloned.1.call-update) | async-done | bytes 6291472 | tf_op jit(solution)/shard_map/all_gather | solution.py:145
  174.7 64.7 %while.17 = (s32[]{:T(128)}, f32[4,4,96]{2,1,0:T(4,128)S(1)}, f32[4,4,96]{2,1,0:T(4,128)S(1)}, f32[96,4,4,128]{3,0,2,1:T(8,128)}, s32[6]{0:T(128)S(1)}, /*index=...) while((s32[]{:T(128)}, f32[4,4,96]{2,1,0:T(4,128)S(1)}, ...), condition=%wide.region_5.6_spmd.clone, body=%wide.region_2.5_spmd.clone.sunk | while | flops 413532864 | bytes 39490572 | solution.py:134
  176.2 1.3 constant_dynamic-slice_fusion.2
  178.2 0.9 copy-done.3
  179.1 2.3 fusion.81
  181.4 2.9 fusion.85
  184.4 1.1 fusion.83
  185.5 0.7 dynamic_slice.32
  187.0 1.3 constant_dynamic-slice_fusion.2
  189.0 0.9 copy-done.3
  189.9 2.3 fusion.81
  192.2 2.9 fusion.85
  195.1 1.1 fusion.83
  196.3 0.7 dynamic_slice.32
  197.8 1.3 constant_dynamic-slice_fusion.2
  199.7 0.9 copy-done.3
  200.6 2.3 fusion.81
  203.0 2.9 fusion.85
  205.9 1.1 fusion.83
  207.1 0.7 dynamic_slice.32
  208.6 1.3 constant_dynamic-slice_fusion.2
  210.5 0.9 copy-done.3
  211.4 2.3 fusion.81
  213.8 2.9 fusion.85
  216.7 1.1 fusion.83
  219.4 1.3 constant_dynamic-slice_fusion.2
  221.3 0.9 copy-done.3
  222.2 2.3 fusion.81
  224.6 2.9 fusion.85
  227.5 1.1 fusion.83
  230.1 1.3 constant_dynamic-slice_fusion.2
  232.1 0.9 copy-done.3
  233.0 2.3 fusion.81
  235.3 2.9 fusion.85
  238.3 1.1 fusion.83
  239.4 1.4 broadcast_divide_fusion
  241.8 3.0 gather_fusion.7
  244.8 2.3 gather.61
  247.1 1.6 select_select_fusion
  248.8 6.3 %all-to-all-start.3 = ((bf16[32,10,2048]{2,1,0:T(8,128)(2,1)}), bf16[32,10,2048]{2,1,0:T(8,128)(2,1)}, u32[]{:S(2)}, u32[]{:S(2)}) async-start(bf16[32,10,2048]{2,1,0:T(8,128)(2,1)} %select_select_fusion), calls=%async_computation.3 | async-start | bytes 4194304 | tf_op jit(solution)/shard_map/all_to_all | solution.py:169
  256.4 48.6 %all-to-all-done.3 = bf16[32,10,2048]{2,1,0:T(8,128)(2,1)} async-done(((bf16[32,10,2048]{2,1,0:T(8,128)(2,1)}), bf16[32,10,2048]{2,1,0:T(8,128)(2,1)}, u32[]{:S(2)}, u32[]{:S(2)}) %all-to-all-start.3) | async-done | bytes 1310752 | tf_op jit(solution)/shard_map/all_to_all | solution.py:169
  305.0 2.5 reshape.584
  307.5 3.0 gather_fusion.8
  310.5 2.5 select_select_fusion.2
  (139 shorter events, 13.8 us)
Async XLA Ops:
  6.5 64.7 %copy-start = (bf16[288,2048]{1,0:T(8,128)(2,1)S(1)}, bf16[288,2048]{1,0:T(8,128)(2,1)}, u32[]{:S(2)}) copy-start(bf16[288,2048]{1,0:T(8,128)(2,1)} %param.7) | copy-start | bytes 3538948
  6.5 22.0 %copy-start.2 = (bf16[288,1024]{1,0:T(8,128)(2,1)S(1)}, bf16[288,1024]{1,0:T(8,128)(2,1)}, u32[]{:S(2)}) copy-start(bf16[288,1024]{1,0:T(8,128)(2,1)} %param.8) | copy-start | bytes 1769476
  17.8 17.8 %all-to-all-start = ((bf16[32,1,10]{2,1,0:T(2,128)(2,1)}), bf16[32,1,10]{2,1,0:T(2,128)(2,1)S(1)}, u32[]{:S(2)}, u32[]{:S(2)}) async-start(bf16[32,1,10]{2,1,0:T(2,128)(2,1)} %copy.20), calls=%async_computation | async-start | bytes 32768 | tf_op jit(solution)/shard_map/all_to_all | solution.py:162
  35.6 33.8 %all-to-all-start.1 = ((bf16[32,10,1024]{2,1,0:T(8,128)(2,1)}), bf16[32,10,1024]{2,1,0:T(8,128)(2,1)S(1)}, u32[]{:S(2)}, u32[]{:S(2)}) async-start(bf16[32,10,1024]{2,1,0:T(8,128)(2,1)} %select_select_fusion.3), calls=%async_computation.1 | async-start | bytes 2097152 | tf_op jit(solution)/shard_map/all_to_all | solution.py:161
  41.8 132.9 %all-gather.2.cloned.1.call-start = ((), (), s32[]{:S(2)}) async-start(), calls=%async_computation.4 | async-start | bytes 6488064 | tf_op jit(solution)/shard_map/all_gather | solution.py:145
  78.3 61.9 %all-to-all-start.2 = ((bf16[32,10,2048]{2,1,0:T(8,128)(2,1)}), bf16[32,10,2048]{2,1,0:T(8,128)(2,1)}, u32[]{:S(2)}, u32[]{:S(2)}) async-start(bf16[32,10,2048]{2,1,0:T(8,128)(2,1)} %select_select_fusion.1), calls=%async_computation.2 | async-start | bytes 4194304 | tf_op jit(solution)/shard_map/all_to_all | solution.py:160
  178.1 1.0 copy-start.3
  178.2 3.2 %copy-start.4 = (f32[96,4,4,128]{3,0,2,1:T(8,128)S(1)}, f32[96,4,4,128]{3,0,2,1:T(8,128)}, u32[]{:S(2)}) copy-start(f32[96,4,4,128]{3,0,2,1:T(8,128)} %get-tuple-element.274) | copy-start | bytes 2359300 | tf_op jit(solution)/shard_map/while
  181.4 2.9 copy-start.1
  184.3 1.1 copy-start.5
  188.9 1.0 copy-start.3
  188.9 3.2 %copy-start.4 = (f32[96,4,4,128]{3,0,2,1:T(8,128)S(1)}, f32[96,4,4,128]{3,0,2,1:T(8,128)}, u32[]{:S(2)}) copy-start(f32[96,4,4,128]{3,0,2,1:T(8,128)} %get-tuple-element.274) | copy-start | bytes 2359300 | tf_op jit(solution)/shard_map/while
  192.2 2.9 copy-start.1
  195.1 1.1 copy-start.5
  199.6 1.0 copy-start.3
  199.7 3.2 %copy-start.4 = (f32[96,4,4,128]{3,0,2,1:T(8,128)S(1)}, f32[96,4,4,128]{3,0,2,1:T(8,128)}, u32[]{:S(2)}) copy-start(f32[96,4,4,128]{3,0,2,1:T(8,128)} %get-tuple-element.274) | copy-start | bytes 2359300 | tf_op jit(solution)/shard_map/while
  203.0 2.9 copy-start.1
  205.9 1.1 copy-start.5
  210.4 1.0 copy-start.3
  210.5 3.2 %copy-start.4 = (f32[96,4,4,128]{3,0,2,1:T(8,128)S(1)}, f32[96,4,4,128]{3,0,2,1:T(8,128)}, u32[]{:S(2)}) copy-start(f32[96,4,4,128]{3,0,2,1:T(8,128)} %get-tuple-element.274) | copy-start | bytes 2359300 | tf_op jit(solution)/shard_map/while
  213.8 2.9 copy-start.1
  216.7 1.1 copy-start.5
  221.2 1.0 copy-start.3
  221.3 3.2 %copy-start.4 = (f32[96,4,4,128]{3,0,2,1:T(8,128)S(1)}, f32[96,4,4,128]{3,0,2,1:T(8,128)}, u32[]{:S(2)}) copy-start(f32[96,4,4,128]{3,0,2,1:T(8,128)} %get-tuple-element.274) | copy-start | bytes 2359300 | tf_op jit(solution)/shard_map/while
  224.5 2.9 copy-start.1
  227.5 1.1 copy-start.5
  232.0 1.0 copy-start.3
  232.1 3.2 %copy-start.4 = (f32[96,4,4,128]{3,0,2,1:T(8,128)S(1)}, f32[96,4,4,128]{3,0,2,1:T(8,128)}, u32[]{:S(2)}) copy-start(f32[96,4,4,128]{3,0,2,1:T(8,128)} %get-tuple-element.274) | copy-start | bytes 2359300 | tf_op jit(solution)/shard_map/while
  235.3 2.9 copy-start.1
  238.3 1.1 copy-start.5
  248.8 56.2 %all-to-all-start.3 = ((bf16[32,10,2048]{2,1,0:T(8,128)(2,1)}), bf16[32,10,2048]{2,1,0:T(8,128)(2,1)}, u32[]{:S(2)}, u32[]{:S(2)}) async-start(bf16[32,10,2048]{2,1,0:T(8,128)(2,1)} %select_select_fusion), calls=%async_computation.3 | async-start | bytes 4194304 | tf_op jit(solution)/shard_map/all_to_all | solution.py:169
Sparse Core Ops, SparseCore 0:
  71.4 103.2 all-gather.1
where the time goes:
time: 321 us; the launch traced here: 320 us
  waiting for transfers between devices  163 us (51%)
  local copies, waits for them, and re-layouts  52.7 us (16%)
  matrix products  31.3 us (10%)
  starting transfers between devices  28.1 us (9%)
  other arithmetic  22.4 us (7%)
  between operations  17.5 us (5%)
  loops' own time  4.95 us (2%)
    all_to_all x1, waiting for transfers between devices, per_device(): lax.all_to_all(packed[0], 'ctx', split_axis=0, concat_axis=0, tiled=True)  56 us
    all_to_all x1, waiting for transfers between devices, per_device(): lax.all_to_all(outgoing, 'ctx', split_axis=0, concat_axis=0, tiled=True)  48.6 us
    all_gather x1, waiting for transfers between devices, attend(): lax.all_gather(kv_bal, 'ctx', axis=0, tiled=True)  30.1 us
    all_to_all x1, waiting for transfers between devices, per_device(): lax.all_to_all(packed[1], 'ctx', split_axis=0, concat_axis=0, tiled=True)  24.6 us
    dot_general x6, matrix products, update(): jnp.einsum('kgqc,ckd->qkgd', weights.astype(jnp.bfloat16), block_value_ro...  17.5 us
    dynamic_slice x18, local copies, waits for them, and re-layouts, fold_piece(): lax.scan(scan_step, running, (blocks, jnp.arange(num_blocks, dtype=jnp.in...  15 us
    dot_general x6, matrix products, update(): jnp.einsum('qkgd,ckd->kgqc', grouped_heads, block_key_rows, preferred_ele...  13.9 us
    gather x6, local copies, waits for them, and re-layouts, pack_forward(): gathered_rows = jnp.take(member, picked, axis=0)  11.4 us
  transfers between devices with their start and end apart: 5, of which 5 were waited for; matrix products, arithmetic and copies ran while one was open for 6% of the time, Pallas kernels for 0%

commit v1 on v0

--- a/solution.py
+++ b/solution.py
@@ -142,7 +142,11 @@
         jnp.zeros((query_row_total, KEY_VALUE_HEADS, group_count, HEAD_SIZE), jnp.float32),
     )
     max_run, total_run, accum = fold_piece(
-        initial, lax.all_gather(kv_bal, "ctx", axis=0, tiled=True), jnp.int32(0)
+        initial,
+        jnp.concatenate(
+            lax.all_to_all(jnp.stack([kv_bal] * lax.axis_size("ctx")), "ctx", 0, 0), axis=0
+        ),
+        jnp.int32(0),
     )
     result = accum / jnp.transpose(total_run, (2, 0, 1))[..., None]
     return result.reshape(query_row_total, QUERY_HEADS * HEAD_SIZE)

time: 321 us -> 404 us (1.26)
  the two profiles are of different devices: /device:TPU:16 before, /device:TPU:2 now
where the time goes in v1:
time: 404 us; the launch traced here: 403 us
  waiting for transfers between devices  248 us (61%)
  local copies, waits for them, and re-layouts  59.7 us (15%)
  starting transfers between devices  32.4 us (8%)
  matrix products  31.3 us (8%)
  other arithmetic  23 us (6%)
  loops' own time  4.61 us (1%)
  between operations  4.45 us (1%)
    all_to_all x1, waiting for transfers between devices, attend(): lax.all_to_all(jnp.stack([kv_bal] * lax.axis_size('ctx')), 'ctx', 0, 0)  135 us
    all_to_all x1, waiting for transfers between devices, per_device(): lax.all_to_all(outgoing, 'ctx', split_axis=0, concat_axis=0, tiled=True)  48.1 us
    all_to_all x1, waiting for transfers between devices, per_device(): lax.all_to_all(packed[0], 'ctx', split_axis=0, concat_axis=0, tiled=True)  39.7 us
    all_to_all x1, waiting for transfers between devices, per_device(): lax.all_to_all(packed[1], 'ctx', split_axis=0, concat_axis=0, tiled=True)  20.5 us
    dot_general x6, matrix products, update(): jnp.einsum('kgqc,ckd->qkgd', weights.astype(jnp.bfloat16), block_value_ro...  17.5 us
    dynamic_slice x18, local copies, waits for them, and re-layouts, fold_piece(): lax.scan(scan_step, running, (blocks, jnp.arange(num_blocks, dtype=jnp.in...  14.7 us
    dot_general x6, matrix products, update(): jnp.einsum('qkgd,ckd->kgqc', grouped_heads, block_key_rows, preferred_ele...  13.9 us
    gather x6, local copies, waits for them, and re-layouts, pack_forward(): gathered_rows = jnp.take(member, picked, axis=0)  11.4 us
  transfers between devices with their start and end apart: 5, of which 5 were waited for; matrix products, arithmetic and copies ran while one was open for 6% of the time, Pallas kernels for 0%

profile of v1, /device:TPU:2, one launch (start us, length us, event | category | flops | bytes accessed | tf_op | source)
XLA Modules:
  0.0 403.0 jit_solution(16762831641831608389)
XLA Ops:
  0.0 1.1 convert_reduce_fusion
  6.7 3.6 gather_fusion.1
  11.8 10.2 %all-to-all-start = ((bf16[32,1,10]{2,1,0:T(2,128)(2,1)}), bf16[32,1,10]{2,1,0:T(2,128)(2,1)S(1)}, u32[]{:S(2)}, u32[]{:S(2)}) async-start(bf16[32,1,10]{2,1,0:T(2,128)(2,1)} %copy.24), calls=%async_computation | async-start | bytes 32768 | tf_op jit(solution)/shard_map/all_to_all | solution.py:166
  22.8 2.1 gather_fusion.3
  25.1 1.2 select_select_fusion.3
  26.3 4.3 %all-to-all-done = bf16[32,1,10]{2,1,0:T(2,128)(2,1)S(1)} async-done(((bf16[32,1,10]{2,1,0:T(2,128)(2,1)}), bf16[32,1,10]{2,1,0:T(2,128)(2,1)S(1)}, u32[]{:S(2)}, u32[]{:S(2)}) %all-to-all-start) | async-done | bytes 672 | tf_op jit(solution)/shard_map/all_to_all | solution.py:166
  30.6 5.5 %all-to-all-start.1 = ((bf16[32,10,1024]{2,1,0:T(8,128)(2,1)}), bf16[32,10,1024]{2,1,0:T(8,128)(2,1)}, u32[]{:S(2)}, u32[]{:S(2)}) async-start(bf16[32,10,1024]{2,1,0:T(8,128)(2,1)} %select_select_fusion.3), calls=%async_computation.1 | async-start | bytes 2097152 | tf_op jit(solution)/shard_map/all_to_all | solution.py:165
  36.2 3.0 gather_fusion.5
  39.2 2.3 gather.57
  41.5 1.7 select_select_fusion.1
  43.2 20.5 %all-to-all-done.1 = bf16[32,10,1024]{2,1,0:T(8,128)(2,1)} async-done(((bf16[32,10,1024]{2,1,0:T(8,128)(2,1)}), bf16[32,10,1024]{2,1,0:T(8,128)(2,1)}, u32[]{:S(2)}, u32[]{:S(2)}) %all-to-all-start.1) | async-done | bytes 655392 | tf_op jit(solution)/shard_map/all_to_all | solution.py:165
  63.7 5.6 %all-to-all-start.3 = ((bf16[32,10,2048]{2,1,0:T(8,128)(2,1)}), bf16[32,10,2048]{2,1,0:T(8,128)(2,1)S(1)}, u32[]{:S(2)}, u32[]{:S(2)}) async-start(bf16[32,10,2048]{2,1,0:T(8,128)(2,1)} %select_select_fusion.1), calls=%async_computation.3 | async-start | bytes 4194304 | tf_op jit(solution)/shard_map/all_to_all | solution.py:164
  69.5 1.2 gather_fusion
  70.9 1.3 gather_fusion.2
  72.2 2.1 reshape.584
  74.3 2.8 gather_fusion.4
  77.1 1.0 broadcast_select_fusion
  78.1 39.7 %all-to-all-done.3 = bf16[32,10,2048]{2,1,0:T(8,128)(2,1)S(1)} async-done(((bf16[32,10,2048]{2,1,0:T(8,128)(2,1)}), bf16[32,10,2048]{2,1,0:T(8,128)(2,1)S(1)}, u32[]{:S(2)}, u32[]{:S(2)}) %all-to-all-start.3) | async-done | bytes 1310752 | tf_op jit(solution)/shard_map/all_to_all | solution.py:164
  117.8 3.5 stack.2
  121.2 6.4 %all-to-all-start.2 = ((bf16[32,96,1024]{2,1,0:T(8,128)(2,1)}), bf16[32,96,1024]{2,1,0:T(8,128)(2,1)}, u32[]{:S(2)}, u32[]{:S(2)}) async-start(bf16[32,96,1024]{2,1,0:T(8,128)(2,1)} %stack.2), calls=%async_computation.2 | async-start | bytes 12582912 | tf_op jit(solution)/shard_map/all_to_all | solution.py:147
  128.0 2.5 reshape.585
  130.5 0.8 gather_fusion.6
  131.6 0.9 copy_select_fusion
  132.5 135.0 %all-to-all-done.2 = bf16[32,96,1024]{2,1,0:T(8,128)(2,1)} async-done(((bf16[32,96,1024]{2,1,0:T(8,128)(2,1)}), bf16[32,96,1024]{2,1,0:T(8,128)(2,1)}, u32[]{:S(2)}, u32[]{:S(2)}) %all-to-all-start.2) | async-done | bytes 6291488 | tf_op jit(solution)/shard_map/all_to_all | solution.py:147
  267.5 64.0 %while.17 = (s32[]{:T(128)}, f32[4,4,96]{2,1,0:T(4,128)S(1)}, f32[4,4,96]{2,1,0:T(4,128)S(1)}, f32[96,4,4,128]{3,0,2,1:T(8,128)}, s32[6]{0:T(128)S(1)}, /*index=...) while((s32[]{:T(128)}, f32[4,4,96]{2,1,0:T(4,128)S(1)}, ...), condition=%wide.region_5.6_spmd.clone, body=%wide.region_2.5_spmd.clone.sunk | while | flops 413532864 | bytes 39490572 | solution.py:134
  268.9 1.3 constant_dynamic-slice_fusion.2
  270.9 0.9 copy-done.3
  271.8 2.3 fusion.81
  274.1 2.9 fusion.85
  277.0 1.1 fusion.83
  279.6 1.3 constant_dynamic-slice_fusion.2
  281.5 0.9 copy-done.3
  282.4 2.3 fusion.81
  284.8 2.9 fusion.85
  287.7 1.1 fusion.83
  290.3 1.3 constant_dynamic-slice_fusion.2
  292.2 0.9 copy-done.3
  293.1 2.3 fusion.81
  295.5 2.9 fusion.85
  298.4 1.1 fusion.83
  300.9 1.3 constant_dynamic-slice_fusion.2
  302.9 0.9 copy-done.3
  303.8 2.3 fusion.81
  306.1 2.9 fusion.85
  309.1 1.1 fusion.83
  311.6 1.3 constant_dynamic-slice_fusion.2
  313.6 0.9 copy-done.3
  314.5 2.3 fusion.81
  316.8 2.9 fusion.85
  319.7 1.1 fusion.83
  322.3 1.3 constant_dynamic-slice_fusion.2
  324.2 0.9 copy-done.3
  325.1 2.3 fusion.81
  327.5 2.9 fusion.85
  330.4 1.1 fusion.83
  331.6 1.4 broadcast_divide_fusion
  333.9 3.0 gather_fusion.7
  337.0 2.3 gather.61
  339.3 1.6 select_select_fusion
  340.9 4.6 %all-to-all-start.4 = ((bf16[32,10,2048]{2,1,0:T(8,128)(2,1)}), bf16[32,10,2048]{2,1,0:T(8,128)(2,1)}, u32[]{:S(2)}, u32[]{:S(2)}) async-start(bf16[32,10,2048]{2,1,0:T(8,128)(2,1)} %select_select_fusion), calls=%async_computation.4 | async-start | bytes 4194304 | tf_op jit(solution)/shard_map/all_to_all | solution.py:173
  346.9 48.1 %all-to-all-done.4 = bf16[32,10,2048]{2,1,0:T(8,128)(2,1)} async-done(((bf16[32,10,2048]{2,1,0:T(8,128)(2,1)}), bf16[32,10,2048]{2,1,0:T(8,128)(2,1)}, u32[]{:S(2)}, u32[]{:S(2)}) %all-to-all-start.4) | async-done | bytes 1310752 | tf_op jit(solution)/shard_map/all_to_all | solution.py:173
  395.1 2.5 reshape.587
  397.6 3.0 gather_fusion.8
  400.6 2.5 select_select_fusion.2
  (141 shorter events, 15.6 us)
Async XLA Ops:
  0.0 36.2 %copy-start = (bf16[288,2048]{1,0:T(8,128)(2,1)S(1)}, bf16[288,2048]{1,0:T(8,128)(2,1)}, u32[]{:S(2)}) copy-start(bf16[288,2048]{1,0:T(8,128)(2,1)} %param.7) | copy-start | bytes 3538948
  0.0 22.8 %copy-start.2 = (bf16[288,1024]{1,0:T(8,128)(2,1)S(1)}, bf16[288,1024]{1,0:T(8,128)(2,1)}, u32[]{:S(2)}) copy-start(bf16[288,1024]{1,0:T(8,128)(2,1)} %param.8) | copy-start | bytes 1769476
  11.8 18.8 %all-to-all-start = ((bf16[32,1,10]{2,1,0:T(2,128)(2,1)}), bf16[32,1,10]{2,1,0:T(2,128)(2,1)S(1)}, u32[]{:S(2)}, u32[]{:S(2)}) async-start(bf16[32,1,10]{2,1,0:T(2,128)(2,1)} %copy.24), calls=%async_computation | async-start | bytes 32768 | tf_op jit(solution)/shard_map/all_to_all | solution.py:166
  30.6 33.1 %all-to-all-start.1 = ((bf16[32,10,1024]{2,1,0:T(8,128)(2,1)}), bf16[32,10,1024]{2,1,0:T(8,128)(2,1)}, u32[]{:S(2)}, u32[]{:S(2)}) async-start(bf16[32,10,1024]{2,1,0:T(8,128)(2,1)} %select_select_fusion.3), calls=%async_computation.1 | async-start | bytes 2097152 | tf_op jit(solution)/shard_map/all_to_all | solution.py:165
  63.7 54.0 %all-to-all-start.3 = ((bf16[32,10,2048]{2,1,0:T(8,128)(2,1)}), bf16[32,10,2048]{2,1,0:T(8,128)(2,1)S(1)}, u32[]{:S(2)}, u32[]{:S(2)}) async-start(bf16[32,10,2048]{2,1,0:T(8,128)(2,1)} %select_select_fusion.1), calls=%async_computation.3 | async-start | bytes 4194304 | tf_op jit(solution)/shard_map/all_to_all | solution.py:164
  117.8 3.5 copy-start.4
  121.2 146.3 %all-to-all-start.2 = ((bf16[32,96,1024]{2,1,0:T(8,128)(2,1)}), bf16[32,96,1024]{2,1,0:T(8,128)(2,1)}, u32[]{:S(2)}, u32[]{:S(2)}) async-start(bf16[32,96,1024]{2,1,0:T(8,128)(2,1)} %stack.2), calls=%async_computation.2 | async-start | bytes 12582912 | tf_op jit(solution)/shard_map/all_to_all | solution.py:147
  270.8 1.0 copy-start.3
  270.8 3.2 copy-start.5
  274.1 2.9 copy-start.1
  277.0 1.1 copy-start.6
  281.4 1.0 copy-start.3
  281.5 3.2 copy-start.5
  284.8 2.9 copy-start.1
  287.7 1.1 copy-start.6
  292.1 1.0 copy-start.3
  292.2 3.2 copy-start.5
  295.4 2.9 copy-start.1
  298.4 1.1 copy-start.6
  302.8 1.0 copy-start.3
  302.9 3.2 copy-start.5
  306.1 2.9 copy-start.1
  309.1 1.1 copy-start.6
  313.5 1.0 copy-start.3
  313.5 3.2 copy-start.5
  316.8 2.9 copy-start.1
  319.7 1.1 copy-start.6
  324.1 1.0 copy-start.3
  324.2 3.2 copy-start.5
  327.5 2.9 copy-start.1
  330.4 1.1 copy-start.6
  340.9 54.2 %all-to-all-start.4 = ((bf16[32,10,2048]{2,1,0:T(8,128)(2,1)}), bf16[32,10,2048]{2,1,0:T(8,128)(2,1)}, u32[]{:S(2)}, u32[]{:S(2)}) async-start(bf16[32,10,2048]{2,1,0:T(8,128)(2,1)} %select_select_fusion), calls=%async_computation.4 | async-start | bytes 4194304 | tf_op jit(solution)/shard_map/all_to_all | solution.py:173
